TPU v7x, 512 devices: a whole 4x4x16 slice. The times are simulated.
512 devices in a mesh: seq: 64 (over x, z), head: 8 (over y, core).
Axes of the slice: x: 4, y: 4, z: 16, core: 2. Of those that a mesh axis runs over, the one named last changes fastest.
Arguments:
- tokens: bfloat16 [16384, 4096], P('seq', 'head'), may hold values from -40 to 40
- queries: bfloat16 [16384, 4096], P('seq', 'head'), may hold values from -6 to 6
- key_rows: bfloat16 [16384, 4096], P('seq', 'head'), may hold values from -6 to 6
- values: bfloat16 [16384, 4096], P('seq', 'head'), may hold values from -6 to 6
- log_decay: float32 [32, 16384], P('head', 'seq'), may hold values from -1 to 0
- head_gain: float32 [4096], P('head'), may hold values from 0.5 to 1.5
- expert_gain: float32 [4096], P('head'), may hold values from 0.5 to 1.5
- route_ids: int32 [16384, 2], P('seq'), may hold values from 0 to 31, all different within a row; in each aligned block of 256 rows (0 to 255, 256 to 511, ...) at most 20 rows name the same one
- route_weight: float32 [16384, 2], P('seq'), may hold values from 0.2 to 1
- expert_in: bfloat16 [64, 4096, 1408], P('seq', 'head'), may hold values from -0.09375 to 0.09375
- expert_out: bfloat16 [64, 704, 4096], P('seq', None, 'head'), may hold values from -0.15625 to 0.15625
Outputs:
- mixed: bfloat16 [16384, 4096], P('seq', 'head')
Inputs may be any that keep to these rules, and one draw needn't show every extreme that they name: `route_ids`: within the rows of one device (aligned blocks of 256 tokens) no expert is named by more than 20 tokens, a bound that some block reaches; a token's two experts differ.
All inputs are finite; a program needn't handle non-finite values.
Results may differ from a plain program's by a relative error of at most 0.015.
Values may be sent and summed in bfloat16 or wider, within the bound.
No kernel may reach another device: no remote copies, remote signals or barrier semaphores. Data moves between devices by JAX's collectives and lax.ppermute only.
A program may use at most 64 MiB of HBM per device.

v0:
```python
import jax
import jax.numpy as jnp
from jax import lax
from jax.sharding import PartitionSpec as P

D = 4096
EXPERTS = 32
CAP = 20
EPSILON = 1e-06


def pack_window(decay, state):
    heads, rows, cols = state.shape
    high = decay.astype(jnp.bfloat16)
    low = (decay - high.astype(jnp.float32)).astype(jnp.bfloat16)
    tail = jnp.broadcast_to(jnp.stack([high, low], axis=1)[:, :, None], (heads, 2, cols))
    return jnp.concatenate([state.astype(jnp.bfloat16), tail], axis=1)


def exclusive_scan(decay, state, axis):
    place = lax.axis_index(axis)
    count = lax.axis_size(axis)
    rows = state.shape[1]
    window_decay = decay
    window_state = state
    before_decay = jnp.ones_like(decay)
    before_state = jnp.zeros_like(state)
    shift = 1
    while shift < count:
        pairs = [(j, j + shift) for j in range(count - shift)]
        got = lax.ppermute(pack_window(window_decay, window_state), axis, pairs)
        valid = place >= shift
        got_state = got[:, :rows, :].astype(jnp.float32)
        got_decay = got[:, rows, 0].astype(jnp.float32) + got[:, rows + 1, 0].astype(jnp.float32)
        got_decay = jnp.where(valid, got_decay, 1.0)
        before_state = before_decay[:, None, None] * got_state + before_state
        before_decay = before_decay * got_decay
        window_state = window_decay[:, None, None] * got_state + window_state
        window_decay = window_decay * got_decay
        shift *= 2
    return before_state


def head_reduce_activate(partial, axis, block_units):
    place = lax.axis_index(axis)
    count = lax.axis_size(axis)
    chips = count // 2
    core = place % 2
    chip = place // 2
    blocks_here, rows, width = partial.shape
    share = rows // count
    pieces = partial.reshape(blocks_here, chips, 2, share, width)
    sibling = [(j, j ^ 1) for j in range(count)]
    kept = lax.dynamic_index_in_dim(pieces, core, 2, False).astype(jnp.float32)
    handed = lax.dynamic_index_in_dim(pieces, 1 - core, 2, False)
    pair_sum = kept + lax.ppermute(handed, axis, sibling).astype(jnp.float32)
    total = lax.dynamic_index_in_dim(pair_sum, chip, 1, False)
    for step in range(1, chips):
        target = (chip + step) % chips
        outgoing = lax.dynamic_index_in_dim(pair_sum, target, 1, False).astype(jnp.bfloat16)
        pairs = [(j, (j + 2 * step) % count) for j in range(count)]
        total = total + lax.ppermute(outgoing, axis, pairs).astype(jnp.float32)
    split = total.reshape(blocks_here, share, width // (2 * block_units), 2, block_units)
    mine = (jax.nn.silu(split[:, :, :, 0]) * split[:, :, :, 1]).astype(jnp.bfloat16)
    mine = mine.reshape(blocks_here, share, width // 2)
    gathered = [mine]
    for step in range(1, chips):
        pairs = [(j, (j + 2 * step) % count) for j in range(count)]
        gathered.append(lax.ppermute(mine, axis, pairs))
    stacked = jnp.stack(gathered, axis=1)
    reverse = stacked[:, ::-1]
    doubled = jnp.concatenate([reverse, reverse], axis=1)
    ordered = lax.dynamic_slice_in_dim(doubled, (chips - 1 - chip) % chips, chips, 1)
    other = lax.ppermute(ordered, axis, sibling)
    three = jnp.stack([ordered, other, ordered], axis=2)
    full = lax.dynamic_slice_in_dim(three, core, 2, 2)
    return full.reshape(blocks_here, rows, width // 2)


def per_device(
    tokens,
    queries,
    key_rows,
    values,
    log_decay,
    head_gain,
    expert_gain,
    route_ids,
    route_weight,
    expert_in,
    expert_out,
):
    parity = lax.axis_index("seq") % 2
    partner = [(j, j ^ 1) for j in range(lax.axis_size("seq"))]
    other_in = lax.ppermute(expert_in, "seq", partner)
    other_out = lax.ppermute(expert_out, "seq", partner)
    length = tokens.shape[0]
    local_width = tokens.shape[1]
    heads_here = log_decay.shape[0]
    head_size = queries.shape[1] // heads_here
    score_scale = head_size ** (-0.5)
    query_heads = queries.reshape(length, heads_here, head_size)
    key_heads = key_rows.reshape(length, heads_here, head_size)
    value_heads = values.reshape(length, heads_here, head_size)
    cumulative = jnp.cumsum(log_decay, axis=1)
    causal = (jnp.arange(length)[:, None] >= jnp.arange(length)[None, :])[None]
    scores = (
        jnp.einsum("thd,shd->hts", query_heads, key_heads, preferred_element_type=jnp.float32)
        * score_scale
    )
    spread = cumulative[:, :, None] - cumulative[:, None, :]
    mixing = jnp.where(causal, scores * jnp.exp(jnp.where(causal, spread, 0.0)), 0.0).astype(
        jnp.bfloat16
    )
    inside = jnp.einsum("hts,shd->thd", mixing, value_heads, preferred_element_type=jnp.float32)
    to_end = jnp.exp(cumulative[:, -1:] - cumulative)
    carried_keys = (key_heads.astype(jnp.float32) * to_end.T[:, :, None]).astype(jnp.bfloat16)
    block_state = jnp.einsum(
        "shd,she->hde", carried_keys, value_heads, preferred_element_type=jnp.float32
    )
    block_decay = jnp.exp(cumulative[:, -1])
    entering = exclusive_scan(block_decay, block_state, "seq")
    entering, other_in = lax.optimization_barrier((entering, other_in))
    from_before = jnp.einsum(
        "thd,hde->the",
        query_heads.astype(jnp.float32),
        entering,
        precision=lax.Precision.HIGHEST,
        preferred_element_type=jnp.float32,
    )
    attended = inside + from_before * (jnp.exp(cumulative).T[:, :, None] * score_scale)
    head_rms = lax.rsqrt(jnp.mean(attended * attended, axis=2, keepdims=True) + EPSILON)
    normed_heads = (attended * head_rms).reshape(length, local_width)
    hidden_state = (tokens.astype(jnp.float32) + normed_heads * head_gain).astype(jnp.bfloat16)
    hidden_wide = hidden_state.astype(jnp.float32)
    local_squares = jnp.sum(hidden_wide * hidden_wide, axis=1)
    total_squares = lax.psum(local_squares, "head")
    inverse_rms = lax.rsqrt(total_squares / D + EPSILON)
    expert_input = (hidden_wide * inverse_rms[:, None] * expert_gain).astype(jnp.bfloat16)
    capacity = CAP
    expert_count = EXPERTS
    flat_ids = route_ids.reshape(-1)
    pair_count = flat_ids.shape[0]
    chosen = (flat_ids[:, None] == jnp.arange(expert_count)[None, :]).astype(jnp.float32)
    strictly_before = (jnp.arange(pair_count)[:, None] > jnp.arange(pair_count)[None, :]).astype(
        jnp.float32
    )
    earlier_counts = jnp.dot(
        strictly_before, chosen, precision=lax.Precision.HIGHEST, preferred_element_type=jnp.float32
    )
    slot_index = jnp.sum(earlier_counts * chosen, axis=1).astype(jnp.int32)
    position = (flat_ids * capacity + slot_index).reshape(length, route_ids.shape[1])
    slot_ids = jnp.arange(expert_count * capacity, dtype=jnp.int32)
    picks = position[None, :, :] == slot_ids[:, None, None]
    dispatch_matrix = jnp.any(picks, axis=2).astype(jnp.bfloat16)
    send_rows = jnp.dot(dispatch_matrix, expert_input, preferred_element_type=jnp.float32).astype(
        jnp.bfloat16
    )
    half = capacity // 2
    block_units = expert_out.shape[1]
    send_buffer = send_rows.reshape(expert_count * 2, 1, half, local_width)
    arrived = lax.all_to_all(send_buffer, "seq", split_axis=0, concat_axis=1, tiled=True)
    blocks_here, sources = (arrived.shape[0], arrived.shape[1])
    flat_rows = arrived.reshape(blocks_here, sources * half, local_width)
    own_sums = jnp.einsum(
        "erd,edh->erh", flat_rows, expert_in, preferred_element_type=jnp.float32
    ).astype(jnp.bfloat16)
    other_sums = jnp.einsum(
        "erd,edh->erh", flat_rows, other_in, preferred_element_type=jnp.float32
    ).astype(jnp.bfloat16)
    partial_sums = jnp.concatenate([own_sums, other_sums], axis=2)
    activated = head_reduce_activate(partial_sums, "head", block_units)
    activated, other_out = lax.optimization_barrier((activated, other_out))
    activated = activated.reshape(blocks_here, sources * half, 2, block_units)
    weight_out = jnp.stack([expert_out, other_out], axis=1)
    summed = jnp.einsum(
        "erkh,ekhd->erd", activated, weight_out, preferred_element_type=jnp.float32
    ).astype(jnp.bfloat16)
    summed = summed.reshape(blocks_here, sources, half, local_width)
    returned = lax.all_to_all(summed, "seq", split_axis=1, concat_axis=0, tiled=True)
    merged = returned.reshape(expert_count, capacity, local_width).astype(jnp.float32)
    merged = merged.reshape(expert_count * capacity, local_width)
    slot_rows = merged[position]
    expert_mix = jnp.sum(slot_rows * route_weight[:, :, None], axis=1)
    return (hidden_wide + expert_mix).astype(jnp.bfloat16)


def solution(mesh):
    return jax.shard_map(
        per_device,
        mesh=mesh,
        in_specs=(
            P("seq", "head"),
            P("seq", "head"),
            P("seq", "head"),
            P("seq", "head"),
            P("head", "seq"),
            P("head"),
            P("head"),
            P("seq", None),
            P("seq", None),
            P("seq", "head", None),
            P("seq", None, "head"),
        ),
        out_specs=P("seq", "head"),
        check_vma=False,
    )
```

profile of v0, /device:TPU:6, one launch (start us, length us, event | category | flops | bytes accessed | tf_op | source)
XLA Modules:
  0.0 340.9 jit_solution(1136357605575012222)
XLA Ops:
  5.1 3.8 %collective-permute-start = (bf16[4,130,128]{2,1,0:T(8,128)(2,1)S(1)}, bf16[4,130,128]{2,1,0:T(8,128)(2,1)S(1)}, u32[]{:S(2)}, u32[]{:S(2)}) collective-permute-start(bf16[4,130,128]{2,1,0:T(8,128)(2,1)S(1)} %pad_maximum_fusion.1), channel_id=1, source_target_pairs={{0,8},{8,16},{16,24},{24,32},{32,40},{40,48},{48,56},{56,64},{64,7... | collective-permute-start | bytes 399368 | tf_op jit(solution)/shard_map/ppermute | solution.py:31
  9.0 11.5 %collective-permute-done = bf16[4,130,128]{2,1,0:T(8,128)(2,1)S(1)} collective-permute-done((bf16[4,130,128]{2,1,0:T(8,128)(2,1)S(1)}, bf16[4,130,128]{2,1,0:T(8,128)(2,1)S(1)}, u32[]{:S(2)}, u32[]{:S(2)}) %collective-permute-start) | collective-permute-done | bytes 133152 | tf_op jit(solution)/shard_map/ppermute | solution.py:31
  22.9 10.1 %collective-permute-done.1 = bf16[4,130,128]{2,1,0:T(8,128)(2,1)S(1)} collective-permute-done((bf16[4,130,128]{2,1,0:T(8,128)(2,1)S(1)}, bf16[4,130,128]{2,1,0:T(8,128)(2,1)S(1)}, u32[]{:S(2)}, u32[]{:S(2)}) %collective-permute-start.1) | collective-permute-done | bytes 133152 | tf_op jit(solution)/shard_map/ppermute | solution.py:31
  35.6 15.3 %collective-permute-done.2 = bf16[4,130,128]{2,1,0:T(8,128)(2,1)S(1)} collective-permute-done((bf16[4,130,128]{2,1,0:T(8,128)(2,1)S(1)}, bf16[4,130,128]{2,1,0:T(8,128)(2,1)S(1)}, u32[]{:S(2)}, u32[]{:S(2)}) %collective-permute-start.2) | collective-permute-done | bytes 133152 | tf_op jit(solution)/shard_map/ppermute | solution.py:31
  53.4 6.7 %collective-permute-start.6 = (bf16[1,512,1408]{2,1,0:T(8,128)(2,1)}, bf16[1,512,1408]{2,1,0:T(8,128)(2,1)}, u32[]{:S(2)}, u32[]{:S(2)}) collective-permute-start(bf16[1,512,1408]{2,1,0:T(8,128)(2,1)} %param.20), channel_id=1, source_target_pairs={{0,8},{8,0},{16,24},{24,16},{32,40},{40,32},{48,56},{56,48},{64,72... | collective-permute-start | bytes 4325384 | tf_op jit(solution)/shard_map/ppermute | solution.py:95
  60.2 11.1 %collective-permute-done.3 = bf16[4,130,128]{2,1,0:T(8,128)(2,1)S(1)} collective-permute-done((bf16[4,130,128]{2,1,0:T(8,128)(2,1)S(1)}, bf16[4,130,128]{2,1,0:T(8,128)(2,1)S(1)}, u32[]{:S(2)}, u32[]{:S(2)}) %collective-permute-start.3) | collective-permute-done | bytes 133152 | tf_op jit(solution)/shard_map/ppermute | solution.py:31
  74.5 4.5 %collective-permute-done.4 = bf16[4,130,128]{2,1,0:T(8,128)(2,1)S(1)} collective-permute-done((bf16[4,130,128]{2,1,0:T(8,128)(2,1)S(1)}, bf16[4,130,128]{2,1,0:T(8,128)(2,1)S(1)}, u32[]{:S(2)}, u32[]{:S(2)}) %collective-permute-start.4) | collective-permute-done | bytes 133152 | tf_op jit(solution)/shard_map/ppermute | solution.py:31
  81.0 6.9 %collective-permute-done.5 = bf16[4,130,128]{2,1,0:T(8,128)(2,1)S(1)} collective-permute-done((bf16[4,130,128]{2,1,0:T(8,128)(2,1)S(1)}, bf16[4,130,128]{2,1,0:T(8,128)(2,1)S(1)}, u32[]{:S(2)}, u32[]{:S(2)}) %collective-permute-start.5) | collective-permute-done | bytes 133152 | tf_op jit(solution)/shard_map/ppermute | solution.py:31
  88.2 8.4 %collective-permute-done.6 = bf16[1,512,1408]{2,1,0:T(8,128)(2,1)} collective-permute-done((bf16[1,512,1408]{2,1,0:T(8,128)(2,1)}, bf16[1,512,1408]{2,1,0:T(8,128)(2,1)}, u32[]{:S(2)}, u32[]{:S(2)}) %collective-permute-start.6) | collective-permute-done | bytes 1441824 | tf_op jit(solution)/shard_map/ppermute | solution.py:95
  97.7 12.4 %psum.7 = f32[256]{0:T(256)S(1)} all-reduce(f32[256]{0:T(256)S(1)} %get-tuple-element.25), channel_id=1, replica_groups=mesh['seq'=64,'head'=8] {'head'}, use_global_device_ids=true, to_apply=%region_6.7 | all-reduce | flops 256 | bytes 2048 | tf_op jit(solution)/shard_map/psum | solution.py:137
  111.7 13.4 %all-to-all-start = ((bf16[64,1,10,512]{3,2,1,0:T(8,128)(2,1)}), bf16[64,1,10,512]{3,2,1,0:T(8,128)(2,1)S(1)}, u32[]{:S(2)}, u32[]{:S(2)}) async-start(bf16[64,1,10,512]{3,2,1,0:T(8,128)(2,1)} %bitcast.8), calls=%async_computation | async-start | bytes 2097152 | tf_op jit(solution)/shard_map/all_to_all | solution.py:162
  125.1 50.7 %all-to-all-done = bf16[64,1,10,512]{3,2,1,0:T(8,128)(2,1)S(1)} async-done(((bf16[64,1,10,512]{3,2,1,0:T(8,128)(2,1)}), bf16[64,1,10,512]{3,2,1,0:T(8,128)(2,1)S(1)}, u32[]{:S(2)}, u32[]{:S(2)}) %all-to-all-start) | async-done | bytes 655392 | tf_op jit(solution)/shard_map/all_to_all | solution.py:162
  185.0 4.0 %collective-permute-done.7 = bf16[1,4,80,2816]{3,2,1,0:T(8,128)(2,1)} collective-permute-done((bf16[1,4,80,2816]{3,2,1,0:T(8,128)(2,1)}, bf16[1,4,80,2816]{3,2,1,0:T(8,128)(2,1)}, u32[]{:S(2)}, u32[]{:S(2)}) %collective-permute-start.7) | collective-permute-done | bytes 1802272 | tf_op jit(solution)/shard_map/ppermute | solution.py:56
  194.8 3.7 %collective-permute-start.9 = (bf16[1,80,2816]{2,1,0:T(8,128)(2,1)S(1)}, bf16[1,80,2816]{2,1,0:T(8,128)(2,1)S(1)}, u32[]{:S(2)}, u32[]{:S(2)}) collective-permute-start(bf16[1,80,2816]{2,1,0:T(8,128)(2,1)S(1)} %get-tuple-element.45), channel_id=1, source_target_pairs={{0,4},{1,5},{2,6},{3,7},{4,0},{5,1},{6,2},{7,3},{8,12},{9,13},{10,... | collective-permute-start | bytes 1351688 | tf_op jit(solution)/shard_map/ppermute | solution.py:62
  198.5 3.4 collective-permute-start.8
  202.0 6.0 %collective-permute-done.10 = bf16[1,80,2816]{2,1,0:T(8,128)(2,1)S(1)} collective-permute-done((bf16[1,80,2816]{2,1,0:T(8,128)(2,1)S(1)}, bf16[1,80,2816]{2,1,0:T(8,128)(2,1)S(1)}, u32[]{:S(2)}, u32[]{:S(2)}) %collective-permute-start.10) | collective-permute-done | bytes 450592 | tf_op jit(solution)/shard_map/ppermute | solution.py:62
  208.0 3.5 %collective-permute-done.9 = bf16[1,80,2816]{2,1,0:T(8,128)(2,1)S(1)} collective-permute-done((bf16[1,80,2816]{2,1,0:T(8,128)(2,1)S(1)}, bf16[1,80,2816]{2,1,0:T(8,128)(2,1)S(1)}, u32[]{:S(2)}, u32[]{:S(2)}) %collective-permute-start.9) | collective-permute-done | bytes 450592 | tf_op jit(solution)/shard_map/ppermute | solution.py:62
  211.5 8.8 %collective-permute-done.8 = bf16[1,80,2816]{2,1,0:T(8,128)(2,1)S(1)} collective-permute-done((bf16[1,80,2816]{2,1,0:T(8,128)(2,1)S(1)}, bf16[1,80,2816]{2,1,0:T(8,128)(2,1)S(1)}, u32[]{:S(2)}, u32[]{:S(2)}) %collective-permute-start.8) | collective-permute-done | bytes 450592 | tf_op jit(solution)/shard_map/ppermute | solution.py:62
  227.3 3.6 %collective-permute-start.12 = (bf16[1,80,1408]{2,1,0:T(8,128)(2,1)S(1)}, bf16[1,80,1408]{2,1,0:T(8,128)(2,1)S(1)}, u32[]{:S(2)}, u32[]{:S(2)}) collective-permute-start(bf16[1,80,1408]{2,1,0:T(8,128)(2,1)S(1)} %multiply_convert_fusion.1), channel_id=1, source_target_pairs={{0,4},{1,5},{2,6},{3,7},{4,0},{5,1},{6,2},{7,3},{8,12},{9,13},{10,... | collective-permute-start | bytes 675848 | tf_op jit(solution)/shard_map/ppermute | solution.py:69
  238.3 4.0 %collective-permute-done.11 = bf16[1,80,1408]{2,1,0:T(8,128)(2,1)S(1)} collective-permute-done((bf16[1,80,1408]{2,1,0:T(8,128)(2,1)S(1)}, bf16[1,80,1408]{2,1,0:T(8,128)(2,1)S(1)}, u32[]{:S(2)}, u32[]{:S(2)}) %collective-permute-start.11) | collective-permute-done | bytes 225312 | tf_op jit(solution)/shard_map/ppermute | solution.py:69
  245.8 5.3 %collective-permute-start.15 = (bf16[1,704,512]{2,1,0:T(8,128)(2,1)}, bf16[1,704,512]{2,1,0:T(8,128)(2,1)}, u32[]{:S(2)}, u32[]{:S(2)}) collective-permute-start(bf16[1,704,512]{2,1,0:T(8,128)(2,1)} %param.21), channel_id=1, source_target_pairs={{0,8},{8,0},{16,24},{24,16},{32,40},{40,32},{48,56},{56,48},{64,72... | collective-permute-start | bytes 2162696 | tf_op jit(solution)/shard_map/ppermute | solution.py:96
  252.7 15.5 %collective-permute-done.15 = bf16[1,704,512]{2,1,0:T(8,128)(2,1)} collective-permute-done((bf16[1,704,512]{2,1,0:T(8,128)(2,1)}, bf16[1,704,512]{2,1,0:T(8,128)(2,1)}, u32[]{:S(2)}, u32[]{:S(2)}) %collective-permute-start.15) | collective-permute-done | bytes 720928 | tf_op jit(solution)/shard_map/ppermute | solution.py:96
  274.8 7.9 %all-to-all-start.1 = ((bf16[1,64,10,512]{3,2,0,1:T(8,128)(2,1)}), bf16[1,64,10,512]{3,2,0,1:T(8,128)(2,1)S(1)}, u32[]{:S(2)}, u32[]{:S(2)}) async-start(bf16[1,64,10,512]{3,2,0,1:T(8,128)(2,1)} %bitcast.30), calls=%async_computation.1 | async-start | bytes 2097152 | tf_op jit(solution)/shard_map/all_to_all | solution.py:180
  283.2 53.2 %all-to-all-done.1 = bf16[1,64,10,512]{3,2,0,1:T(8,128)(2,1)S(1)} async-done(((bf16[1,64,10,512]{3,2,0,1:T(8,128)(2,1)}), bf16[1,64,10,512]{3,2,0,1:T(8,128)(2,1)S(1)}, u32[]{:S(2)}, u32[]{:S(2)}) %all-to-all-start.1) | async-done | bytes 655392 | tf_op jit(solution)/shard_map/all_to_all | solution.py:180
  (146 shorter events, 66.3 us)
Async XLA Ops:
  0.0 73.1 %copy-start = (bf16[256,512]{1,0:T(8,128)(2,1)S(1)}, bf16[256,512]{1,0:T(8,128)(2,1)}, u32[]{:S(2)}) copy-start(bf16[256,512]{1,0:T(8,128)(2,1)} %param.12) | copy-start | bytes 786436
  5.1 15.3 %collective-permute-start = (bf16[4,130,128]{2,1,0:T(8,128)(2,1)S(1)}, bf16[4,130,128]{2,1,0:T(8,128)(2,1)S(1)}, u32[]{:S(2)}, u32[]{:S(2)}) collective-permute-start(bf16[4,130,128]{2,1,0:T(8,128)(2,1)S(1)} %pad_maximum_fusion.1), channel_id=1, source_target_pairs={{0,8},{8,16},{16,24},{24,32},{32,40},{40,48},{48,56},{56,64},{64,7... | collective-permute-start | bytes 399368 | tf_op jit(solution)/shard_map/ppermute | solution.py:31
  20.8 52.3 %copy-start.3 = (bf16[256,512]{1,0:T(8,128)(2,1)S(1)}, bf16[256,512]{1,0:T(8,128)(2,1)}, u32[]{:S(2)}) copy-start(bf16[256,512]{1,0:T(8,128)(2,1)} %param.14) | copy-start | bytes 786436
  20.9 12.2 %collective-permute-start.1 = (bf16[4,130,128]{2,1,0:T(8,128)(2,1)S(1)}, bf16[4,130,128]{2,1,0:T(8,128)(2,1)S(1)}, u32[]{:S(2)}, u32[]{:S(2)}) collective-permute-start(bf16[4,130,128]{2,1,0:T(8,128)(2,1)S(1)} %pad_maximum_fusion.2), channel_id=1, source_target_pairs={{0,16},{8,24},{16,32},{24,40},{32,48},{40,56},{48,64},{56,72},{64,... | collective-permute-start | bytes 399368 | tf_op jit(solution)/shard_map/ppermute | solution.py:31
  33.7 17.3 %collective-permute-start.2 = (bf16[4,130,128]{2,1,0:T(8,128)(2,1)S(1)}, bf16[4,130,128]{2,1,0:T(8,128)(2,1)S(1)}, u32[]{:S(2)}, u32[]{:S(2)}) collective-permute-start(bf16[4,130,128]{2,1,0:T(8,128)(2,1)S(1)} %pad_maximum_fusion.3), channel_id=1, source_target_pairs={{0,32},{8,40},{16,48},{24,56},{32,64},{40,72},{48,80},{56,88},{64,... | collective-permute-start | bytes 399368 | tf_op jit(solution)/shard_map/ppermute | solution.py:31
  51.5 19.8 %collective-permute-start.3 = (bf16[4,130,128]{2,1,0:T(8,128)(2,1)S(1)}, bf16[4,130,128]{2,1,0:T(8,128)(2,1)S(1)}, u32[]{:S(2)}, u32[]{:S(2)}) collective-permute-start(bf16[4,130,128]{2,1,0:T(8,128)(2,1)S(1)} %pad_maximum_fusion.4), channel_id=1, source_target_pairs={{0,64},{8,72},{16,80},{24,88},{32,96},{40,104},{48,112},{56,120},{... | collective-permute-start | bytes 399368 | tf_op jit(solution)/shard_map/ppermute | solution.py:31
  53.4 43.2 %collective-permute-start.6 = (bf16[1,512,1408]{2,1,0:T(8,128)(2,1)}, bf16[1,512,1408]{2,1,0:T(8,128)(2,1)}, u32[]{:S(2)}, u32[]{:S(2)}) collective-permute-start(bf16[1,512,1408]{2,1,0:T(8,128)(2,1)} %param.20), channel_id=1, source_target_pairs={{0,8},{8,0},{16,24},{24,16},{32,40},{40,32},{48,56},{56,48},{64,72... | collective-permute-start | bytes 4325384 | tf_op jit(solution)/shard_map/ppermute | solution.py:95
  71.7 2.0 copy-start.5
  71.8 7.2 %collective-permute-start.4 = (bf16[4,130,128]{2,1,0:T(8,128)(2,1)S(1)}, bf16[4,130,128]{2,1,0:T(8,128)(2,1)S(1)}, u32[]{:S(2)}, u32[]{:S(2)}) collective-permute-start(bf16[4,130,128]{2,1,0:T(8,128)(2,1)S(1)} %pad_maximum_fusion.5), channel_id=1, source_target_pairs={{0,128},{8,136},{16,144},{24,152},{32,160},{40,168},{48,176},{56,1... | collective-permute-start | bytes 399368 | tf_op jit(solution)/shard_map/ppermute | solution.py:31
  79.5 8.5 %collective-permute-start.5 = (bf16[4,130,128]{2,1,0:T(8,128)(2,1)S(1)}, bf16[4,130,128]{2,1,0:T(8,128)(2,1)S(1)}, u32[]{:S(2)}, u32[]{:S(2)}) collective-permute-start(bf16[4,130,128]{2,1,0:T(8,128)(2,1)S(1)} %pad_maximum_fusion.6), channel_id=1, source_target_pairs={{0,256},{8,264},{16,272},{24,280},{32,288},{40,296},{48,304},{56,3... | collective-permute-start | bytes 399368 | tf_op jit(solution)/shard_map/ppermute | solution.py:31
  97.0 13.1 %copy-start.8 = (f32[512]{0:T(512)S(1)}, f32[512]{0:T(512)}, u32[]{:S(2)}) copy-start(f32[512]{0:T(512)} %param.17) | copy-start | bytes 6148
  111.7 64.1 %all-to-all-start = ((bf16[64,1,10,512]{3,2,1,0:T(8,128)(2,1)}), bf16[64,1,10,512]{3,2,1,0:T(8,128)(2,1)S(1)}, u32[]{:S(2)}, u32[]{:S(2)}) async-start(bf16[64,1,10,512]{3,2,1,0:T(8,128)(2,1)} %bitcast.8), calls=%async_computation | async-start | bytes 2097152 | tf_op jit(solution)/shard_map/all_to_all | solution.py:162
  181.2 1.8 copy-start.2
  183.0 6.0 %collective-permute-start.7 = (bf16[1,4,80,2816]{3,2,1,0:T(8,128)(2,1)}, bf16[1,4,80,2816]{3,2,1,0:T(8,128)(2,1)}, u32[]{:S(2)}, u32[]{:S(2)}) collective-permute-start(bf16[1,4,80,2816]{3,2,1,0:T(8,128)(2,1)} %fusion.3), channel_id=1, source_target_pairs={{0,1},{1,0},{2,3},{3,2},{4,5},{5,4},{6,7},{7,6},{8,9},{9,8},{10,11... | collective-permute-start | bytes 5406728 | tf_op jit(solution)/shard_map/ppermute | solution.py:56
  192.9 15.1 %collective-permute-start.10 = (bf16[1,80,2816]{2,1,0:T(8,128)(2,1)S(1)}, bf16[1,80,2816]{2,1,0:T(8,128)(2,1)S(1)}, u32[]{:S(2)}, u32[]{:S(2)}) collective-permute-start(bf16[1,80,2816]{2,1,0:T(8,128)(2,1)S(1)} %get-tuple-element.44), channel_id=1, source_target_pairs={{0,6},{1,7},{2,0},{3,1},{4,2},{5,3},{6,4},{7,5},{8,14},{9,15},{10,... | collective-permute-start | bytes 1351688 | tf_op jit(solution)/shard_map/ppermute | solution.py:62
  194.8 16.6 %collective-permute-start.9 = (bf16[1,80,2816]{2,1,0:T(8,128)(2,1)S(1)}, bf16[1,80,2816]{2,1,0:T(8,128)(2,1)S(1)}, u32[]{:S(2)}, u32[]{:S(2)}) collective-permute-start(bf16[1,80,2816]{2,1,0:T(8,128)(2,1)S(1)} %get-tuple-element.45), channel_id=1, source_target_pairs={{0,4},{1,5},{2,6},{3,7},{4,0},{5,1},{6,2},{7,3},{8,12},{9,13},{10,... | collective-permute-start | bytes 1351688 | tf_op jit(solution)/shard_map/ppermute | solution.py:62
  198.5 21.8 %collective-permute-start.8 = (bf16[1,80,2816]{2,1,0:T(8,128)(2,1)S(1)}, bf16[1,80,2816]{2,1,0:T(8,128)(2,1)S(1)}, u32[]{:S(2)}, u32[]{:S(2)}) collective-permute-start(bf16[1,80,2816]{2,1,0:T(8,128)(2,1)S(1)} %get-tuple-element.43), channel_id=1, source_target_pairs={{0,2},{1,3},{2,4},{3,5},{4,6},{5,7},{6,0},{7,1},{8,10},{9,11},{10,... | collective-permute-start | bytes 1351688 | tf_op jit(solution)/shard_map/ppermute | solution.py:62
  224.8 10.3 %collective-permute-start.13 = (bf16[1,80,1408]{2,1,0:T(8,128)(2,1)S(1)}, bf16[1,80,1408]{2,1,0:T(8,128)(2,1)S(1)}, u32[]{:S(2)}, u32[]{:S(2)}) collective-permute-start(bf16[1,80,1408]{2,1,0:T(8,128)(2,1)S(1)} %multiply_convert_fusion.1), channel_id=1, source_target_pairs={{0,6},{1,7},{2,0},{3,1},{4,2},{5,3},{6,4},{7,5},{8,14},{9,15},{10,... | collective-permute-start | bytes 675848 | tf_op jit(solution)/shard_map/ppermute | solution.py:69
  227.3 11.0 %collective-permute-start.12 = (bf16[1,80,1408]{2,1,0:T(8,128)(2,1)S(1)}, bf16[1,80,1408]{2,1,0:T(8,128)(2,1)S(1)}, u32[]{:S(2)}, u32[]{:S(2)}) collective-permute-start(bf16[1,80,1408]{2,1,0:T(8,128)(2,1)S(1)} %multiply_convert_fusion.1), channel_id=1, source_target_pairs={{0,4},{1,5},{2,6},{3,7},{4,0},{5,1},{6,2},{7,3},{8,12},{9,13},{10,... | collective-permute-start | bytes 675848 | tf_op jit(solution)/shard_map/ppermute | solution.py:69
  230.9 11.5 %collective-permute-start.11 = (bf16[1,80,1408]{2,1,0:T(8,128)(2,1)S(1)}, bf16[1,80,1408]{2,1,0:T(8,128)(2,1)S(1)}, u32[]{:S(2)}, u32[]{:S(2)}) collective-permute-start(bf16[1,80,1408]{2,1,0:T(8,128)(2,1)S(1)} %multiply_convert_fusion.1), channel_id=1, source_target_pairs={{0,2},{1,3},{2,4},{3,5},{4,6},{5,7},{6,0},{7,1},{8,10},{9,11},{10,... | collective-permute-start | bytes 675848 | tf_op jit(solution)/shard_map/ppermute | solution.py:69
  243.9 7.6 %collective-permute-start.14 = (bf16[1,4,80,1408]{3,2,1,0:T(8,128)(2,1)}, bf16[1,4,80,1408]{3,2,1,0:T(8,128)(2,1)S(1)}, u32[]{:S(2)}, u32[]{:S(2)}) collective-permute-start(bf16[1,4,80,1408]{3,2,1,0:T(8,128)(2,1)} %fusion.25), channel_id=1, source_target_pairs={{0,1},{1,0},{2,3},{3,2},{4,5},{5,4},{6,7},{7,6},{8,9},{9,8},{10,11... | collective-permute-start | bytes 2703368 | tf_op jit(solution)/shard_map/ppermute | solution.py:74
  245.8 22.4 %collective-permute-start.15 = (bf16[1,704,512]{2,1,0:T(8,128)(2,1)}, bf16[1,704,512]{2,1,0:T(8,128)(2,1)}, u32[]{:S(2)}, u32[]{:S(2)}) collective-permute-start(bf16[1,704,512]{2,1,0:T(8,128)(2,1)} %param.21), channel_id=1, source_target_pairs={{0,8},{8,0},{16,24},{24,16},{32,40},{40,32},{48,56},{56,48},{64,72... | collective-permute-start | bytes 2162696 | tf_op jit(solution)/shard_map/ppermute | solution.py:96
  273.6 9.4 %copy-start.7 = (f32[256,2]{0,1:T(2,128)S(1)}, f32[256,2]{0,1:T(2,128)}, u32[]{:S(2)}) copy-start(f32[256,2]{0,1:T(2,128)} %param.19) | copy-start | bytes 6148
  274.8 61.5 %all-to-all-start.1 = ((bf16[1,64,10,512]{3,2,0,1:T(8,128)(2,1)}), bf16[1,64,10,512]{3,2,0,1:T(8,128)(2,1)S(1)}, u32[]{:S(2)}, u32[]{:S(2)}) async-start(bf16[1,64,10,512]{3,2,0,1:T(8,128)(2,1)} %bitcast.30), calls=%async_computation.1 | async-start | bytes 2097152 | tf_op jit(solution)/shard_map/all_to_all | solution.py:180
  (3 other events, 3.7 us)
where the time goes:
time: 342 us; the launch traced here: 341 us
  waiting for transfers between devices  217 us (63%)
  starting transfers between devices  67.1 us (20%)
  local copies, waits for them, and re-layouts  18.2 us (5%)
  other arithmetic  13.8 us (4%)
  blocking collectives  12.4 us (4%)
  matrix products  11.1 us (3%)
    ppermute x6, waiting for transfers between devices, exclusive_scan(): got = lax.ppermute(pack_window(window_decay, window_state), axis, pairs)  59.5 us
    all_to_all x1, waiting for transfers between devices, per_device(): lax.all_to_all(summed, 'seq', split_axis=1, concat_axis=0, tiled=True)  53.2 us
    all_to_all x1, waiting for transfers between devices, per_device(): lax.all_to_all(send_buffer, 'seq', split_axis=0, concat_axis=1, tiled=True)  50.7 us
    ppermute x3, waiting for transfers between devices, head_reduce_activate(): total = total + lax.ppermute(outgoing, axis, pairs).astype(jnp.float32)  18.4 us
    ppermute x1, waiting for transfers between devices, per_device(): other_out = lax.ppermute(expert_out, 'seq', partner)  15.5 us
    all_to_all x1, starting transfers between devices, per_device(): lax.all_to_all(send_buffer, 'seq', split_axis=0, concat_axis=1, tiled=True)  13.4 us
    psum x1, blocking collectives, per_device(): total_squares = lax.psum(local_squares, 'head')  12.4 us
    ppermute x6, starting transfers between devices, exclusive_scan(): got = lax.ppermute(pack_window(window_decay, window_state), axis, pairs)  12.2 us
  transfers between devices with their start and end apart: 18, of which 17 were waited for; matrix products, arithmetic and copies ran while one was open for 2% of the time, Pallas kernels for 0%

commit v1 on v0

--- a/solution.py
+++ b/solution.py
@@ -134,7 +134,7 @@
     hidden_state = (tokens.astype(jnp.float32) + normed_heads * head_gain).astype(jnp.bfloat16)
     hidden_wide = hidden_state.astype(jnp.float32)
     local_squares = jnp.sum(hidden_wide * hidden_wide, axis=1)
-    total_squares = lax.psum(local_squares, "head")
+    total_squares = jax.lax.all_gather(local_squares, axis_name="head").sum(axis=0)
     inverse_rms = lax.rsqrt(total_squares / D + EPSILON)
     expert_input = (hidden_wide * inverse_rms[:, None] * expert_gain).astype(jnp.bfloat16)
     capacity = CAP

time: 342 us -> 339 us (level)
  waiting for transfers between devices: 217 us -> 223 us
  starting transfers between devices: 67.1 us -> 61.2 us
    psum x1 -> x0, blocking collectives: 12.4 us -> none  [per_device(): total_squares = lax.psum(local_squares, 'head')]
    all_gather x0 -> x1, blocking collectives: none -> 9.78 us  [per_device(): jax.lax.all_gather(local_squares, axis_name='head').sum(axis=0)]
    all_to_all x1, waiting for transfers between devices: 50.7 us -> 54.4 us  [per_device(): lax.all_to_all(send_buffer, 'seq', split_axis=0, concat_axis=1, tiled=True)]
where the time goes in v1:
time: 339 us; the launch traced here: 338 us
  waiting for transfers between devices  223 us (66%)
  starting transfers between devices  61.2 us (18%)
  local copies, waits for them, and re-layouts  18.2 us (5%)
  other arithmetic  13.9 us (4%)
  matrix products  11.1 us (3%)
  blocking collectives  9.78 us (3%)
    ppermute x6, waiting for transfers between devices, exclusive_scan(): got = lax.ppermute(pack_window(window_decay, window_state), axis, pairs)  59.5 us
    all_to_all x1, waiting for transfers between devices, per_device(): lax.all_to_all(send_buffer, 'seq', split_axis=0, concat_axis=1, tiled=True)  54.4 us
    all_to_all x1, waiting for transfers between devices, per_device(): lax.all_to_all(summed, 'seq', split_axis=1, concat_axis=0, tiled=True)  53.2 us
    ppermute x3, waiting for transfers between devices, head_reduce_activate(): total = total + lax.ppermute(outgoing, axis, pairs).astype(jnp.float32)  19.2 us
    ppermute x1, waiting for transfers between devices, per_device(): other_out = lax.ppermute(expert_out, 'seq', partner)  16.1 us
    all_to_all x1, starting transfers between devices, per_device(): lax.all_to_all(send_buffer, 'seq', split_axis=0, concat_axis=1, tiled=True)  12.2 us
    ppermute x6, starting transfers between devices, exclusive_scan(): got = lax.ppermute(pack_window(window_decay, window_state), axis, pairs)  12.2 us
    all_gather x1, blocking collectives, per_device(): jax.lax.all_gather(local_squares, axis_name='head').sum(axis=0)  9.78 us
  transfers between devices with their start and end apart: 18, of which 17 were waited for; matrix products, arithmetic and copies ran while one was open for 2% of the time, Pallas kernels for 0%

profile of v1, /device:TPU:6, one launch (start us, length us, event | category | flops | bytes accessed | tf_op | source)
XLA Modules:
  0.0 338.0 jit_solution(936194519044418843)
XLA Ops:
  5.1 3.8 %collective-permute-start = (bf16[4,130,128]{2,1,0:T(8,128)(2,1)S(1)}, bf16[4,130,128]{2,1,0:T(8,128)(2,1)S(1)}, u32[]{:S(2)}, u32[]{:S(2)}) collective-permute-start(bf16[4,130,128]{2,1,0:T(8,128)(2,1)S(1)} %pad_maximum_fusion.1), channel_id=1, source_target_pairs={{0,8},{8,16},{16,24},{24,32},{32,40},{40,48},{48,56},{56,64},{64,7... | collective-permute-start | bytes 399368 | tf_op jit(solution)/shard_map/ppermute | solution.py:31
  9.0 11.5 %collective-permute-done = bf16[4,130,128]{2,1,0:T(8,128)(2,1)S(1)} collective-permute-done((bf16[4,130,128]{2,1,0:T(8,128)(2,1)S(1)}, bf16[4,130,128]{2,1,0:T(8,128)(2,1)S(1)}, u32[]{:S(2)}, u32[]{:S(2)}) %collective-permute-start) | collective-permute-done | bytes 133152 | tf_op jit(solution)/shard_map/ppermute | solution.py:31
  22.9 10.1 %collective-permute-done.1 = bf16[4,130,128]{2,1,0:T(8,128)(2,1)S(1)} collective-permute-done((bf16[4,130,128]{2,1,0:T(8,128)(2,1)S(1)}, bf16[4,130,128]{2,1,0:T(8,128)(2,1)S(1)}, u32[]{:S(2)}, u32[]{:S(2)}) %collective-permute-start.1) | collective-permute-done | bytes 133152 | tf_op jit(solution)/shard_map/ppermute | solution.py:31
  35.6 15.3 %collective-permute-done.2 = bf16[4,130,128]{2,1,0:T(8,128)(2,1)S(1)} collective-permute-done((bf16[4,130,128]{2,1,0:T(8,128)(2,1)S(1)}, bf16[4,130,128]{2,1,0:T(8,128)(2,1)S(1)}, u32[]{:S(2)}, u32[]{:S(2)}) %collective-permute-start.2) | collective-permute-done | bytes 133152 | tf_op jit(solution)/shard_map/ppermute | solution.py:31
  53.4 6.7 %collective-permute-start.6 = (bf16[1,512,1408]{2,1,0:T(8,128)(2,1)}, bf16[1,512,1408]{2,1,0:T(8,128)(2,1)}, u32[]{:S(2)}, u32[]{:S(2)}) collective-permute-start(bf16[1,512,1408]{2,1,0:T(8,128)(2,1)} %param.20), channel_id=1, source_target_pairs={{0,8},{8,0},{16,24},{24,16},{32,40},{40,32},{48,56},{56,48},{64,72... | collective-permute-start | bytes 4325384 | tf_op jit(solution)/shard_map/ppermute | solution.py:95
  60.2 11.1 %collective-permute-done.3 = bf16[4,130,128]{2,1,0:T(8,128)(2,1)S(1)} collective-permute-done((bf16[4,130,128]{2,1,0:T(8,128)(2,1)S(1)}, bf16[4,130,128]{2,1,0:T(8,128)(2,1)S(1)}, u32[]{:S(2)}, u32[]{:S(2)}) %collective-permute-start.3) | collective-permute-done | bytes 133152 | tf_op jit(solution)/shard_map/ppermute | solution.py:31
  74.5 4.5 %collective-permute-done.4 = bf16[4,130,128]{2,1,0:T(8,128)(2,1)S(1)} collective-permute-done((bf16[4,130,128]{2,1,0:T(8,128)(2,1)S(1)}, bf16[4,130,128]{2,1,0:T(8,128)(2,1)S(1)}, u32[]{:S(2)}, u32[]{:S(2)}) %collective-permute-start.4) | collective-permute-done | bytes 133152 | tf_op jit(solution)/shard_map/ppermute | solution.py:31
  81.0 6.9 %collective-permute-done.5 = bf16[4,130,128]{2,1,0:T(8,128)(2,1)S(1)} collective-permute-done((bf16[4,130,128]{2,1,0:T(8,128)(2,1)S(1)}, bf16[4,130,128]{2,1,0:T(8,128)(2,1)S(1)}, u32[]{:S(2)}, u32[]{:S(2)}) %collective-permute-start.5) | collective-permute-done | bytes 133152 | tf_op jit(solution)/shard_map/ppermute | solution.py:31
  88.2 8.4 %collective-permute-done.6 = bf16[1,512,1408]{2,1,0:T(8,128)(2,1)} collective-permute-done((bf16[1,512,1408]{2,1,0:T(8,128)(2,1)}, bf16[1,512,1408]{2,1,0:T(8,128)(2,1)}, u32[]{:S(2)}, u32[]{:S(2)}) %collective-permute-start.6) | collective-permute-done | bytes 1441824 | tf_op jit(solution)/shard_map/ppermute | solution.py:95
  97.7 9.8 %all-gather.1 = f32[8,1,256]{2,1,0:T(1,128)S(1)} all-gather(f32[1,1,256]{2,1,0:T(1,128)S(1)} %bitcast.167), channel_id=2, replica_groups=mesh['seq'=64,'head'=8] {'head'}, dimensions={0}, use_global_device_ids=true | all-gather | bytes 9216 | tf_op jit(solution)/shard_map/all_gather | solution.py:137
  109.1 12.2 %all-to-all-start = ((bf16[64,1,10,512]{3,2,1,0:T(8,128)(2,1)}), bf16[64,1,10,512]{3,2,1,0:T(8,128)(2,1)S(1)}, u32[]{:S(2)}, u32[]{:S(2)}) async-start(bf16[64,1,10,512]{3,2,1,0:T(8,128)(2,1)} %bitcast.9), calls=%async_computation | async-start | bytes 2097152 | tf_op jit(solution)/shard_map/all_to_all | solution.py:162
  121.3 54.4 %all-to-all-done = bf16[64,1,10,512]{3,2,1,0:T(8,128)(2,1)S(1)} async-done(((bf16[64,1,10,512]{3,2,1,0:T(8,128)(2,1)}), bf16[64,1,10,512]{3,2,1,0:T(8,128)(2,1)S(1)}, u32[]{:S(2)}, u32[]{:S(2)}) %all-to-all-start) | async-done | bytes 655392 | tf_op jit(solution)/shard_map/all_to_all | solution.py:162
  184.9 4.0 %collective-permute-done.7 = bf16[1,4,80,2816]{3,2,1,0:T(8,128)(2,1)} collective-permute-done((bf16[1,4,80,2816]{3,2,1,0:T(8,128)(2,1)}, bf16[1,4,80,2816]{3,2,1,0:T(8,128)(2,1)}, u32[]{:S(2)}, u32[]{:S(2)}) %collective-permute-start.7) | collective-permute-done | bytes 1802272 | tf_op jit(solution)/shard_map/ppermute | solution.py:56
  194.8 3.4 %collective-permute-start.9 = (bf16[1,80,2816]{2,1,0:T(8,128)(2,1)S(1)}, bf16[1,80,2816]{2,1,0:T(8,128)(2,1)S(1)}, u32[]{:S(2)}, u32[]{:S(2)}) collective-permute-start(bf16[1,80,2816]{2,1,0:T(8,128)(2,1)S(1)} %get-tuple-element.45), channel_id=1, source_target_pairs={{0,4},{1,5},{2,6},{3,7},{4,0},{5,1},{6,2},{7,3},{8,12},{9,13},{10,... | collective-permute-start | bytes 1351688 | tf_op jit(solution)/shard_map/ppermute | solution.py:62
  201.0 6.9 %collective-permute-done.10 = bf16[1,80,2816]{2,1,0:T(8,128)(2,1)S(1)} collective-permute-done((bf16[1,80,2816]{2,1,0:T(8,128)(2,1)S(1)}, bf16[1,80,2816]{2,1,0:T(8,128)(2,1)S(1)}, u32[]{:S(2)}, u32[]{:S(2)}) %collective-permute-start.10) | collective-permute-done | bytes 450592 | tf_op jit(solution)/shard_map/ppermute | solution.py:62
  207.9 3.5 %collective-permute-done.9 = bf16[1,80,2816]{2,1,0:T(8,128)(2,1)S(1)} collective-permute-done((bf16[1,80,2816]{2,1,0:T(8,128)(2,1)S(1)}, bf16[1,80,2816]{2,1,0:T(8,128)(2,1)S(1)}, u32[]{:S(2)}, u32[]{:S(2)}) %collective-permute-start.9) | collective-permute-done | bytes 450592 | tf_op jit(solution)/shard_map/ppermute | solution.py:62
  211.4 8.8 %collective-permute-done.8 = bf16[1,80,2816]{2,1,0:T(8,128)(2,1)S(1)} collective-permute-done((bf16[1,80,2816]{2,1,0:T(8,128)(2,1)S(1)}, bf16[1,80,2816]{2,1,0:T(8,128)(2,1)S(1)}, u32[]{:S(2)}, u32[]{:S(2)}) %collective-permute-start.8) | collective-permute-done | bytes 450592 | tf_op jit(solution)/shard_map/ppermute | solution.py:62
  227.2 3.2 collective-permute-start.12
  235.0 3.3 collective-permute-done.12
  238.3 4.0 %collective-permute-done.11 = bf16[1,80,1408]{2,1,0:T(8,128)(2,1)S(1)} collective-permute-done((bf16[1,80,1408]{2,1,0:T(8,128)(2,1)S(1)}, bf16[1,80,1408]{2,1,0:T(8,128)(2,1)S(1)}, u32[]{:S(2)}, u32[]{:S(2)}) %collective-permute-start.11) | collective-permute-done | bytes 225312 | tf_op jit(solution)/shard_map/ppermute | solution.py:69
  250.4 16.1 %collective-permute-done.15 = bf16[1,704,512]{2,1,0:T(8,128)(2,1)} collective-permute-done((bf16[1,704,512]{2,1,0:T(8,128)(2,1)}, bf16[1,704,512]{2,1,0:T(8,128)(2,1)}, u32[]{:S(2)}, u32[]{:S(2)}) %collective-permute-start.15) | collective-permute-done | bytes 720928 | tf_op jit(solution)/shard_map/ppermute | solution.py:96
  268.8 3.1 fusion.14
  273.1 6.7 %all-to-all-start.1 = ((bf16[1,64,10,512]{3,2,0,1:T(8,128)(2,1)}), bf16[1,64,10,512]{3,2,0,1:T(8,128)(2,1)S(1)}, u32[]{:S(2)}, u32[]{:S(2)}) async-start(bf16[1,64,10,512]{3,2,0,1:T(8,128)(2,1)} %bitcast.31), calls=%async_computation.1 | async-start | bytes 2097152 | tf_op jit(solution)/shard_map/all_to_all | solution.py:180
  280.2 53.2 %all-to-all-done.1 = bf16[1,64,10,512]{3,2,0,1:T(8,128)(2,1)S(1)} async-done(((bf16[1,64,10,512]{3,2,0,1:T(8,128)(2,1)}), bf16[1,64,10,512]{3,2,0,1:T(8,128)(2,1)S(1)}, u32[]{:S(2)}, u32[]{:S(2)}) %all-to-all-start.1) | async-done | bytes 655392 | tf_op jit(solution)/shard_map/all_to_all | solution.py:180
  (147 shorter events, 66.2 us)
Async XLA Ops:
  0.0 73.1 %copy-start = (bf16[256,512]{1,0:T(8,128)(2,1)S(1)}, bf16[256,512]{1,0:T(8,128)(2,1)}, u32[]{:S(2)}) copy-start(bf16[256,512]{1,0:T(8,128)(2,1)} %param.12) | copy-start | bytes 786436
  5.1 15.3 %collective-permute-start = (bf16[4,130,128]{2,1,0:T(8,128)(2,1)S(1)}, bf16[4,130,128]{2,1,0:T(8,128)(2,1)S(1)}, u32[]{:S(2)}, u32[]{:S(2)}) collective-permute-start(bf16[4,130,128]{2,1,0:T(8,128)(2,1)S(1)} %pad_maximum_fusion.1), channel_id=1, source_target_pairs={{0,8},{8,16},{16,24},{24,32},{32,40},{40,48},{48,56},{56,64},{64,7... | collective-permute-start | bytes 399368 | tf_op jit(solution)/shard_map/ppermute | solution.py:31
  20.8 52.3 %copy-start.3 = (bf16[256,512]{1,0:T(8,128)(2,1)S(1)}, bf16[256,512]{1,0:T(8,128)(2,1)}, u32[]{:S(2)}) copy-start(bf16[256,512]{1,0:T(8,128)(2,1)} %param.14) | copy-start | bytes 786436
  20.9 12.2 %collective-permute-start.1 = (bf16[4,130,128]{2,1,0:T(8,128)(2,1)S(1)}, bf16[4,130,128]{2,1,0:T(8,128)(2,1)S(1)}, u32[]{:S(2)}, u32[]{:S(2)}) collective-permute-start(bf16[4,130,128]{2,1,0:T(8,128)(2,1)S(1)} %pad_maximum_fusion.2), channel_id=1, source_target_pairs={{0,16},{8,24},{16,32},{24,40},{32,48},{40,56},{48,64},{56,72},{64,... | collective-permute-start | bytes 399368 | tf_op jit(solution)/shard_map/ppermute | solution.py:31
  33.7 17.3 %collective-permute-start.2 = (bf16[4,130,128]{2,1,0:T(8,128)(2,1)S(1)}, bf16[4,130,128]{2,1,0:T(8,128)(2,1)S(1)}, u32[]{:S(2)}, u32[]{:S(2)}) collective-permute-start(bf16[4,130,128]{2,1,0:T(8,128)(2,1)S(1)} %pad_maximum_fusion.3), channel_id=1, source_target_pairs={{0,32},{8,40},{16,48},{24,56},{32,64},{40,72},{48,80},{56,88},{64,... | collective-permute-start | bytes 399368 | tf_op jit(solution)/shard_map/ppermute | solution.py:31
  51.5 19.8 %collective-permute-start.3 = (bf16[4,130,128]{2,1,0:T(8,128)(2,1)S(1)}, bf16[4,130,128]{2,1,0:T(8,128)(2,1)S(1)}, u32[]{:S(2)}, u32[]{:S(2)}) collective-permute-start(bf16[4,130,128]{2,1,0:T(8,128)(2,1)S(1)} %pad_maximum_fusion.4), channel_id=1, source_target_pairs={{0,64},{8,72},{16,80},{24,88},{32,96},{40,104},{48,112},{56,120},{... | collective-permute-start | bytes 399368 | tf_op jit(solution)/shard_map/ppermute | solution.py:31
  53.4 43.2 %collective-permute-start.6 = (bf16[1,512,1408]{2,1,0:T(8,128)(2,1)}, bf16[1,512,1408]{2,1,0:T(8,128)(2,1)}, u32[]{:S(2)}, u32[]{:S(2)}) collective-permute-start(bf16[1,512,1408]{2,1,0:T(8,128)(2,1)} %param.20), channel_id=1, source_target_pairs={{0,8},{8,0},{16,24},{24,16},{32,40},{40,32},{48,56},{56,48},{64,72... | collective-permute-start | bytes 4325384 | tf_op jit(solution)/shard_map/ppermute | solution.py:95
  71.7 2.0 copy-start.5
  71.8 7.2 %collective-permute-start.4 = (bf16[4,130,128]{2,1,0:T(8,128)(2,1)S(1)}, bf16[4,130,128]{2,1,0:T(8,128)(2,1)S(1)}, u32[]{:S(2)}, u32[]{:S(2)}) collective-permute-start(bf16[4,130,128]{2,1,0:T(8,128)(2,1)S(1)} %pad_maximum_fusion.5), channel_id=1, source_target_pairs={{0,128},{8,136},{16,144},{24,152},{32,160},{40,168},{48,176},{56,1... | collective-permute-start | bytes 399368 | tf_op jit(solution)/shard_map/ppermute | solution.py:31
  79.5 8.5 %collective-permute-start.5 = (bf16[4,130,128]{2,1,0:T(8,128)(2,1)S(1)}, bf16[4,130,128]{2,1,0:T(8,128)(2,1)S(1)}, u32[]{:S(2)}, u32[]{:S(2)}) collective-permute-start(bf16[4,130,128]{2,1,0:T(8,128)(2,1)S(1)} %pad_maximum_fusion.6), channel_id=1, source_target_pairs={{0,256},{8,264},{16,272},{24,280},{32,288},{40,296},{48,304},{56,3... | collective-permute-start | bytes 399368 | tf_op jit(solution)/shard_map/ppermute | solution.py:31
  97.0 10.5 %copy-start.8 = (f32[512]{0:T(512)S(1)}, f32[512]{0:T(512)}, u32[]{:S(2)}) copy-start(f32[512]{0:T(512)} %param.17) | copy-start | bytes 6148
  109.1 66.6 %all-to-all-start = ((bf16[64,1,10,512]{3,2,1,0:T(8,128)(2,1)}), bf16[64,1,10,512]{3,2,1,0:T(8,128)(2,1)S(1)}, u32[]{:S(2)}, u32[]{:S(2)}) async-start(bf16[64,1,10,512]{3,2,1,0:T(8,128)(2,1)} %bitcast.9), calls=%async_computation | async-start | bytes 2097152 | tf_op jit(solution)/shard_map/all_to_all | solution.py:162
  181.1 1.8 copy-start.2
  182.9 6.0 %collective-permute-start.7 = (bf16[1,4,80,2816]{3,2,1,0:T(8,128)(2,1)}, bf16[1,4,80,2816]{3,2,1,0:T(8,128)(2,1)}, u32[]{:S(2)}, u32[]{:S(2)}) collective-permute-start(bf16[1,4,80,2816]{3,2,1,0:T(8,128)(2,1)} %fusion.3), channel_id=1, source_target_pairs={{0,1},{1,0},{2,3},{3,2},{4,5},{5,4},{6,7},{7,6},{8,9},{9,8},{10,11... | collective-permute-start | bytes 5406728 | tf_op jit(solution)/shard_map/ppermute | solution.py:56
  192.9 15.1 %collective-permute-start.10 = (bf16[1,80,2816]{2,1,0:T(8,128)(2,1)S(1)}, bf16[1,80,2816]{2,1,0:T(8,128)(2,1)S(1)}, u32[]{:S(2)}, u32[]{:S(2)}) collective-permute-start(bf16[1,80,2816]{2,1,0:T(8,128)(2,1)S(1)} %get-tuple-element.44), channel_id=1, source_target_pairs={{0,6},{1,7},{2,0},{3,1},{4,2},{5,3},{6,4},{7,5},{8,14},{9,15},{10,... | collective-permute-start | bytes 1351688 | tf_op jit(solution)/shard_map/ppermute | solution.py:62
  194.8 16.6 %collective-permute-start.9 = (bf16[1,80,2816]{2,1,0:T(8,128)(2,1)S(1)}, bf16[1,80,2816]{2,1,0:T(8,128)(2,1)S(1)}, u32[]{:S(2)}, u32[]{:S(2)}) collective-permute-start(bf16[1,80,2816]{2,1,0:T(8,128)(2,1)S(1)} %get-tuple-element.45), channel_id=1, source_target_pairs={{0,4},{1,5},{2,6},{3,7},{4,0},{5,1},{6,2},{7,3},{8,12},{9,13},{10,... | collective-permute-start | bytes 1351688 | tf_op jit(solution)/shard_map/ppermute | solution.py:62
  198.2 22.0 %collective-permute-start.8 = (bf16[1,80,2816]{2,1,0:T(8,128)(2,1)S(1)}, bf16[1,80,2816]{2,1,0:T(8,128)(2,1)S(1)}, u32[]{:S(2)}, u32[]{:S(2)}) collective-permute-start(bf16[1,80,2816]{2,1,0:T(8,128)(2,1)S(1)} %get-tuple-element.43), channel_id=1, source_target_pairs={{0,2},{1,3},{2,4},{3,5},{4,6},{5,7},{6,0},{7,1},{8,10},{9,11},{10,... | collective-permute-start | bytes 1351688 | tf_op jit(solution)/shard_map/ppermute | solution.py:62
  224.7 10.3 %collective-permute-start.13 = (bf16[1,80,1408]{2,1,0:T(8,128)(2,1)S(1)}, bf16[1,80,1408]{2,1,0:T(8,128)(2,1)S(1)}, u32[]{:S(2)}, u32[]{:S(2)}) collective-permute-start(bf16[1,80,1408]{2,1,0:T(8,128)(2,1)S(1)} %multiply_convert_fusion.1), channel_id=1, source_target_pairs={{0,6},{1,7},{2,0},{3,1},{4,2},{5,3},{6,4},{7,5},{8,14},{9,15},{10,... | collective-permute-start | bytes 675848 | tf_op jit(solution)/shard_map/ppermute | solution.py:69
  227.2 11.0 %collective-permute-start.12 = (bf16[1,80,1408]{2,1,0:T(8,128)(2,1)S(1)}, bf16[1,80,1408]{2,1,0:T(8,128)(2,1)S(1)}, u32[]{:S(2)}, u32[]{:S(2)}) collective-permute-start(bf16[1,80,1408]{2,1,0:T(8,128)(2,1)S(1)} %multiply_convert_fusion.1), channel_id=1, source_target_pairs={{0,4},{1,5},{2,6},{3,7},{4,0},{5,1},{6,2},{7,3},{8,12},{9,13},{10,... | collective-permute-start | bytes 675848 | tf_op jit(solution)/shard_map/ppermute | solution.py:69
  230.4 11.9 %collective-permute-start.11 = (bf16[1,80,1408]{2,1,0:T(8,128)(2,1)S(1)}, bf16[1,80,1408]{2,1,0:T(8,128)(2,1)S(1)}, u32[]{:S(2)}, u32[]{:S(2)}) collective-permute-start(bf16[1,80,1408]{2,1,0:T(8,128)(2,1)S(1)} %multiply_convert_fusion.1), channel_id=1, source_target_pairs={{0,2},{1,3},{2,4},{3,5},{4,6},{5,7},{6,0},{7,1},{8,10},{9,11},{10,... | collective-permute-start | bytes 675848 | tf_op jit(solution)/shard_map/ppermute | solution.py:69
  243.8 5.4 %collective-permute-start.14 = (bf16[1,4,80,1408]{3,2,1,0:T(8,128)(2,1)}, bf16[1,4,80,1408]{3,2,1,0:T(8,128)(2,1)S(1)}, u32[]{:S(2)}, u32[]{:S(2)}) collective-permute-start(bf16[1,4,80,1408]{3,2,1,0:T(8,128)(2,1)} %fusion.25), channel_id=1, source_target_pairs={{0,1},{1,0},{2,3},{3,2},{4,5},{5,4},{6,7},{7,6},{8,9},{9,8},{10,11... | collective-permute-start | bytes 2703368 | tf_op jit(solution)/shard_map/ppermute | solution.py:74
  245.8 20.8 %collective-permute-start.15 = (bf16[1,704,512]{2,1,0:T(8,128)(2,1)}, bf16[1,704,512]{2,1,0:T(8,128)(2,1)}, u32[]{:S(2)}, u32[]{:S(2)}) collective-permute-start(bf16[1,704,512]{2,1,0:T(8,128)(2,1)} %param.21), channel_id=1, source_target_pairs={{0,8},{8,0},{16,24},{24,16},{32,40},{40,32},{48,56},{56,48},{64,72... | collective-permute-start | bytes 2162696 | tf_op jit(solution)/shard_map/ppermute | solution.py:96
  271.9 8.2 %copy-start.7 = (f32[256,2]{0,1:T(2,128)S(1)}, f32[256,2]{0,1:T(2,128)}, u32[]{:S(2)}) copy-start(f32[256,2]{0,1:T(2,128)} %param.19) | copy-start | bytes 6148
  273.1 60.3 %all-to-all-start.1 = ((bf16[1,64,10,512]{3,2,0,1:T(8,128)(2,1)}), bf16[1,64,10,512]{3,2,0,1:T(8,128)(2,1)S(1)}, u32[]{:S(2)}, u32[]{:S(2)}) async-start(bf16[1,64,10,512]{3,2,0,1:T(8,128)(2,1)} %bitcast.31), calls=%async_computation.1 | async-start | bytes 2097152 | tf_op jit(solution)/shard_map/all_to_all | solution.py:180
  (3 other events, 3.7 us)
